TPU v7x, 256 devices: a whole 4x4x8 slice. The times are simulated.
256 devices in a mesh: dp: 8 (over y, x_hi), expert: 8 (over z), tensor: 4 (over x_lo, core).
Axes of the slice: x: 4 (x_hi: 2, x_lo: 2; x = x_hi * 2 + x_lo), y: 4, z: 8, core: 2. Of those that a mesh axis runs over, the one named last changes fastest.
Arguments:
- tokens: bfloat16 [4096, 2048], P(('dp', 'expert', 'tensor')), may hold values from -6 to 6
- cotangent: bfloat16 [4096, 2048], P(('dp', 'expert', 'tensor')), may hold values from -3 to 3
- routes: int32 [4096, 2], P(('dp', 'expert', 'tensor')), may hold values from 0 to 7, all different within a row; in each aligned block of 16 rows (0 to 15, 16 to 31, ...) at most 5 rows name the same one
- weight_codes: int32 [4096, 2], P(('dp', 'expert', 'tensor')), may hold values from 16 to 256
- dense_gate: bfloat16 [2048, 8192], P('expert', ('dp', 'tensor')), may hold values from -0.125 to 0.125
- dense_up: bfloat16 [2048, 8192], P('expert', ('dp', 'tensor')), may hold values from -0.125 to 0.125
- dense_down_t: bfloat16 [2048, 8192], P('expert', ('dp', 'tensor')), may hold values from -0.0625 to 0.0625
Outputs:
- mixed: bfloat16 [4096, 2048], P(('dp', 'expert', 'tensor'))
- input_grad: bfloat16 [4096, 2048], P(('dp', 'expert', 'tensor'))
- grad_gate: bfloat16 [8, 2048, 8192], P('expert', None, ('dp', 'tensor'))
- grad_up: bfloat16 [8, 2048, 8192], P('expert', None, ('dp', 'tensor'))
- grad_down_t: bfloat16 [8, 2048, 8192], P('expert', None, ('dp', 'tensor'))
Inputs may be any that keep to these rules, and one draw needn't show every extreme that they name: `routes`: each row names two different experts; the rows of one device name each expert at most 5 times.
All inputs are finite; a program needn't handle non-finite values.
Results may differ from a plain program's by a relative error of at most 0.02.
Values may be sent and summed in bfloat16 or wider, within the bound.
No kernel may reach another device: no remote copies, remote signals or barrier semaphores. Data moves between devices by JAX's collectives and lax.ppermute only.
A program may use at most 128 MiB of HBM per device.

v0:
```python
import jax
import jax.numpy as jnp
from jax import lax
from jax.sharding import PartitionSpec as P

GROUP = ("dp", "tensor")


def silu_parts(gate_pre):
    sigmoid_val = jax.nn.sigmoid(gate_pre)
    return (gate_pre * sigmoid_val, sigmoid_val * (1.0 + gate_pre * (1.0 - sigmoid_val)))


def contract_rows(left_side, right_side):
    return lax.dot_general(
        left_side, right_side, (((0,), (0,)), ((), ())), preferred_element_type=jnp.float32
    )


def contract_cols(left_side, right_side):
    return lax.dot_general(
        left_side, right_side, (((1,), (1,)), ((), ())), preferred_element_type=jnp.float32
    )


def forward_parts(rows_x, gate_cols, up_cols):
    gate_pre = jnp.dot(rows_x, gate_cols, preferred_element_type=jnp.float32)
    up_pre = jnp.dot(rows_x, up_cols, preferred_element_type=jnp.float32)
    activation, act_slope = silu_parts(gate_pre)
    hidden = (activation * up_pre).astype(jnp.bfloat16)
    return (up_pre, activation, act_slope, hidden)


def grad_parts(scaled, down_cols, up_pre, activation, act_slope):
    hidden_grad = jnp.dot(scaled, down_cols, preferred_element_type=jnp.float32)
    gate_grad = (hidden_grad * up_pre * act_slope).astype(jnp.bfloat16)
    up_grad = (hidden_grad * activation).astype(jnp.bfloat16)
    return (gate_grad, up_grad)


def shards(tokens, cotangent, routes, weight_codes, dense_gate, dense_up, dense_down_t):
    experts = lax.axis_size("expert")
    count_tok, model_width = tokens.shape
    hid = dense_gate.shape[1]
    capacity = 5 * count_tok // (2 * experts)
    slots_here = experts * capacity
    stacked = jnp.concatenate([dense_gate, dense_up, dense_down_t], axis=1)
    full_cols = lax.all_gather(stacked, "expert", axis=0, tiled=True)
    gate_cols = full_cols[:, :hid]
    up_cols = full_cols[:, hid : 2 * hid]
    down_cols = full_cols[:, 2 * hid :]
    gate_up_cols = full_cols[:, : 2 * hid]
    code_cols = jnp.zeros((count_tok, 128), jnp.bfloat16)
    code_cols = code_cols.at[:, 0:2].set(weight_codes.astype(jnp.bfloat16))
    home = jnp.concatenate([tokens, cotangent, code_cols], axis=1)
    plane = lax.all_gather(home, GROUP, axis=0, tiled=True)
    plane_x = plane[:, :model_width]
    plane_dy = plane[:, model_width : 2 * model_width].astype(jnp.float32)
    plane_scale = plane[:, 2 * model_width : 2 * model_width + 2].astype(jnp.float32) / 256.0
    up_pre, activation, act_slope, hidden = forward_parts(plane_x, gate_cols, up_cols)
    out_term = contract_cols(hidden, down_cols).astype(jnp.bfloat16)
    grad_term = jnp.zeros(out_term.shape, jnp.float32)
    for which in range(2):
        scaled = (plane_scale[:, which : which + 1] * plane_dy).astype(jnp.bfloat16)
        gate_grad, up_grad = grad_parts(scaled, down_cols, up_pre, activation, act_slope)
        grad_term = grad_term + contract_cols(
            jnp.concatenate([gate_grad, up_grad], axis=1), gate_up_cols
        )
    terms = jnp.concatenate([out_term, grad_term.astype(jnp.bfloat16)], axis=1)
    summed = lax.psum_scatter(terms, GROUP, scatter_dimension=0, tiled=True)
    expert_out = summed[:, :model_width].astype(jnp.float32)
    code_scale = weight_codes.astype(jnp.float32) / 256.0
    mixed = (code_scale[:, 0:1] * expert_out + code_scale[:, 1:2] * expert_out).astype(jnp.bfloat16)
    input_grad = summed[:, model_width:]
    flat_route = routes.reshape(-1)
    flat_scale = weight_codes.reshape(-1).astype(jnp.float32) / 256.0
    onehot = (flat_route[:, None] == jnp.arange(experts, dtype=jnp.int32)[None, :]).astype(
        jnp.int32
    )
    earlier = jnp.cumsum(onehot, axis=0) - onehot
    slot_of = flat_route * capacity + jnp.sum(earlier * onehot, axis=1)
    placed = (slot_of[None, :] == jnp.arange(slots_here, dtype=jnp.int32)[:, None]).astype(
        jnp.bfloat16
    )
    flat_x = jnp.repeat(tokens, 2, axis=0)
    flat_scaled = (
        flat_scale[:, None] * jnp.repeat(cotangent, 2, axis=0).astype(jnp.float32)
    ).astype(jnp.bfloat16)
    send_x = jnp.dot(placed, flat_x, preferred_element_type=jnp.float32).astype(jnp.bfloat16)
    send_s = jnp.dot(placed, flat_scaled, preferred_element_type=jnp.float32).astype(jnp.bfloat16)
    send = jnp.stack(
        [
            send_x.reshape(experts, capacity, model_width),
            send_s.reshape(experts, capacity, model_width),
        ],
        axis=1,
    )
    got = lax.all_to_all(send, "expert", split_axis=0, concat_axis=0, tiled=True)
    got = jnp.transpose(got, (1, 0, 2, 3))
    rows = lax.all_gather(got, GROUP, axis=1, tiled=True)
    rows_x = rows[0].reshape(-1, model_width)
    rows_s = rows[1].reshape(-1, model_width)
    r_up, r_act, r_slope, r_hidden = forward_parts(rows_x, gate_cols, up_cols)
    r_gate, r_upg = grad_parts(rows_s, down_cols, r_up, r_act, r_slope)
    grad_gate = contract_rows(rows_x, r_gate).astype(jnp.bfloat16)[None]
    grad_up = contract_rows(rows_x, r_upg).astype(jnp.bfloat16)[None]
    grad_down_t = contract_rows(rows_s, r_hidden).astype(jnp.bfloat16)[None]
    return (mixed, input_grad, grad_gate, grad_up, grad_down_t)


def solution(mesh):
    rows = P(("dp", "expert", "tensor"), None)
    weights = P("expert", ("dp", "tensor"))
    grads = P("expert", None, ("dp", "tensor"))
    return jax.shard_map(
        shards,
        mesh=mesh,
        in_specs=(rows, rows, rows, rows, weights, weights, weights),
        out_specs=(rows, rows, grads, grads, grads),
        check_vma=False,
    )
```

profile of v0, /device:TPU:1, one launch (start us, length us, event | category | flops | bytes accessed | tf_op | source)
XLA Modules:
  0.0 376.8 jit_solution(17290189949668021922)
XLA Ops:
  7.9 1.3 broadcast_select_fusion
  9.3 1.5 fusion.43
  10.9 1.8 pad_maximum_fusion.2
  12.8 54.0 %all-gather.4.cloned.1.call-done = bf16[512,4224]{1,0:T(8,128)(2,1)} async-done(((bf16[16,4224]{1,0:T(8,128)(2,1)}), bf16[512,4224]{1,0:T(8,128)(2,1)}) %all-gather.4.cloned.1.call-update) | async-done | bytes 4325392 | tf_op jit(solution)/shard_map/all_gather | solution.py:56
  68.0 44.9 %all-gather.6.cloned.1.call-done = bf16[2048,768]{1,0:T(8,128)(2,1)} async-done(((bf16[256,768]{1,0:T(8,128)(2,1)}), bf16[2048,768]{1,0:T(8,128)(2,1)}) %all-gather.6.cloned.1.call-update) | async-done | bytes 3145744 | tf_op jit(solution)/shard_map/all_gather | solution.py:48
  112.9 2.8 fusion.16
  115.8 2.5 fusion.18
  123.9 2.6 pad_maximum_fusion
  128.9 1.9 convolution_convert_fusion.4
  134.3 1.7 stack_reshape.6
  137.4 15.5 %all_to_all.5 = bf16[8,2,5,2048]{3,1,2,0:T(2,128)(2,1)} all-to-all(bf16[8,2,5,2048]{3,1,2,0:T(2,128)(2,1)S(1)} %copy.25), channel_id=1, replica_groups=mesh['dp'=8,'expert'=8,'tensor'=4] {'expert'}, dimensions={0} | all-to-all | bytes 655360 | tf_op jit(solution)/shard_map/all_to_all | solution.py:98
  152.9 60.5 %reduce-scatter.2.cloned.1.call-done = bf16[16,4096]{1,0:T(8,128)(2,1)} async-done(((bf16[512,4096]{1,0:T(8,128)(2,1)}), bf16[16,4096]{1,0:T(8,128)(2,1)}) %reduce-scatter.2.cloned.1.call-update) | async-done | bytes 131088 | tf_op jit(solution)/shard_map/reduce_scatter | solution.py:70
  213.4 1.5 slice.86
  214.9 1.5 multiply_convert_fusion.14
  216.5 64.0 %all-gather.8.cloned.1.call-done = bf16[2,256,5,2048]{3,0,2,1:T(2,128)(2,1)} async-done(((bf16[2,8,5,2048]{3,0,2,1:T(2,128)(2,1)}), bf16[2,256,5,2048]{3,0,2,1:T(2,128)(2,1)}) %all-gather.8.cloned.1.call-update) | async-done | bytes 10485776 | tf_op jit(solution)/shard_map/all_gather | solution.py:100
  280.5 53.6 %slice_reduce_fusion = (bf16[256,5,2048]{2,1,0:T(8,128)(2,1)}, bf16[256,5,2048]{2,1,0:T(8,128)(2,1)}) fusion(bf16[2,256,5,2048]{3,0,2,1:T(2,128)(2,1)} %all-gather.8.cloned.1.call-done), kind=kLoop, calls=%fused_computation | loop fusion | bytes 20971520 | tf_op jit(solution)/shard_map/slice | solution.py:102
  334.1 10.0 %reshape_squeeze.6 = bf16[1280,2048]{1,0:T(8,128)(2,1)} reshape(bf16[256,5,2048]{2,1,0:T(8,128)(2,1)} %get-tuple-element.18) | data formatting | bytes 10485760 | tf_op jit(solution)/shard_map/reshape;squeeze | solution.py:101
  344.2 10.0 %reshape_squeeze.7 = bf16[1280,2048]{1,0:T(8,128)(2,1)} reshape(bf16[256,5,2048]{2,1,0:T(8,128)(2,1)} %get-tuple-element.17) | data formatting | bytes 10485760 | tf_op jit(solution)/shard_map/reshape;squeeze | solution.py:102
  354.2 4.2 %fusion.24 = f32[1280,256]{1,0:T(8,128)S(1)} fusion(bf16[1280,2048]{1,0:T(8,128)(2,1)} %reshape_squeeze.6, bf16[2048,768]{1,0:T(8,128)(2,1)S(1)} %copy-done.1), kind=kOutput, calls=%fused_computation.38 | convolution fusion | flops 1342177280 | bytes 7602176 | tf_op jit(solution)/shard_map/dot_general | solution.py:27
  358.4 1.6 fusion.21
  360.0 2.9 fusion.4
  362.8 1.6 fusion.27
  364.4 2.9 fusion.3
  367.3 3.0 fusion.2
  (54 shorter events, 15.2 us)
Async XLA Ops:
  7.2 59.6 %all-gather.4.cloned.1.call-start = ((), (), s32[]{:S(2)}) async-start(), calls=%async_computation.2 | async-start | bytes 4460544 | tf_op jit(solution)/shard_map/all_gather | solution.py:56
  10.8 102.1 %all-gather.6.cloned.1.call-start = ((), (), s32[]{:S(2)}) async-start(), calls=%async_computation.3 | async-start | bytes 3538944 | tf_op jit(solution)/shard_map/all_gather | solution.py:48
  12.7 200.7 %reduce-scatter.2.cloned.1.call-start = ((), (), s32[]{:S(2)}) async-start(), calls=%async_computation.4 | async-start | bytes 4325376 | tf_op jit(solution)/shard_map/reduce_scatter | solution.py:70
  112.9 2.9 copy-start.1
  115.8 2.9 copy-start.5
  126.5 0.7 copy-start.6
  126.5 0.9 copy-start.4
  126.5 1.0 copy-start.2
  126.5 5.2 %copy-start.3 = (bf16[16,2048]{1,0:T(8,128)(2,1)S(1)}, bf16[16,2048]{1,0:T(8,128)(2,1)}, u32[]{:S(2)}) copy-start(bf16[16,2048]{1,0:T(8,128)(2,1)} %param.9) | copy-start | bytes 196612
  126.5 154.0 %all-gather.8.cloned.1.call-start = ((), (), s32[]{:S(2)}) async-start(), calls=%async_computation.5 | async-start | bytes 10813440 | tf_op jit(solution)/shard_map/all_gather | solution.py:100
  354.2 4.2 %copy-start = (bf16[1280,2048]{1,0:T(8,128)(2,1)S(1)}, bf16[1280,2048]{1,0:T(8,128)(2,1)}, u32[]{:S(2)}) copy-start(bf16[1280,2048]{1,0:T(8,128)(2,1)} %reshape_squeeze.6) | copy-start | bytes 15728644
  354.2 5.8 %slice-start = ((s8[5242880]{0:T(1024)(128)(4,1)}), s8[4194304]{0:T(1024)(128)(4,1)S(1)}, s32[]{:S(2)}) async-start(s8[5242880]{0:T(1024)(128)(4,1)} %bitcast.16), calls=%async_computation.6 | async-start | bytes 8388608
  358.4 1.6 slice-start.1
Sparse Core Ops, SparseCore 0:
  11.2 55.5 all-gather.3
  69.1 43.7 all-gather.5
  126.7 86.7 reduce-scatter.1
  216.2 64.2 all-gather.7
where the time goes:
time: 378 us; the launch traced here: 377 us
  waiting for transfers between devices  224 us (59%)
  local copies, waits for them, and re-layouts  82.6 us (22%)
  matrix products  29.2 us (8%)
  blocking collectives  15.5 us (4%)
  between operations  14 us (4%)
  other arithmetic  11.7 us (3%)
    all_gather x1, waiting for transfers between devices, shards(): rows = lax.all_gather(got, GROUP, axis=1, tiled=True)  64 us
    reduce_scatter x1, waiting for transfers between devices, shards(): summed = lax.psum_scatter(terms, GROUP, scatter_dimension=0, tiled=True)  60.5 us
    all_gather x1, waiting for transfers between devices, shards(): plane = lax.all_gather(home, GROUP, axis=0, tiled=True)  54 us
    slice x1, local copies, waits for them, and re-layouts, shards(): rows_s = rows[1].reshape(-1, model_width)  53.6 us
    all_gather x1, waiting for transfers between devices, shards(): full_cols = lax.all_gather(stacked, 'expert', axis=0, tiled=True)  44.9 us
    all_to_all x1, blocking collectives, shards(): lax.all_to_all(send, 'expert', split_axis=0, concat_axis=0, tiled=True)  15.5 us
    another operation x1, local copies, waits for them, and re-layouts, shards(): rows_x = rows[0].reshape(-1, model_width)  10 us
    another operation x1, local copies, waits for them, and re-layouts, shards(): rows_s = rows[1].reshape(-1, model_width)  10 us
  transfers between devices with their start and end apart: 4, of which 4 were waited for; matrix products, arithmetic and copies ran while one was open for 4% of the time, Pallas kernels for 0%

commit v1 on v0

--- a/solution.py
+++ b/solution.py
@@ -45,7 +45,9 @@
     capacity = 5 * count_tok // (2 * experts)
     slots_here = experts * capacity
     stacked = jnp.concatenate([dense_gate, dense_up, dense_down_t], axis=1)
-    full_cols = lax.all_gather(stacked, "expert", axis=0, tiled=True)
+    full_cols = jnp.concatenate(
+        lax.all_to_all(jnp.stack([stacked] * lax.axis_size("expert")), "expert", 0, 0), axis=0
+    )
     gate_cols = full_cols[:, :hid]
     up_cols = full_cols[:, hid : 2 * hid]
     down_cols = full_cols[:, 2 * hid :]

time: 378 us -> 365 us (0.966)
  waiting for transfers between devices: 224 us -> 194 us
  starting transfers between devices: 0.16 us -> 9.13 us
  matrix products: 29.2 us -> 34.5 us
    all_gather x1 -> x0, waiting for transfers between devices: 44.9 us -> none  [shards(): full_cols = lax.all_gather(stacked, 'expert', axis=0, tiled=True)]
    all_to_all x0 -> x1, waiting for transfers between devices: none -> 29.1 us  [shards(): lax.all_to_all(jnp.stack([stacked] * lax.axis_size('expert')), 'expert',...]
    all_gather x1, waiting for transfers between devices: 54 us -> 43.9 us  [shards(): plane = lax.all_gather(home, GROUP, axis=0, tiled=True)]
    all_to_all x0 -> x1, starting transfers between devices: none -> 9.01 us  [shards(): lax.all_to_all(jnp.stack([stacked] * lax.axis_size('expert')), 'expert',...]
  transfers between devices with their start and end apart: 4 -> 4, of which waited for: 4 -> 4; matrix products, arithmetic and copies ran while one was open for 4% -> 5% of each run, Pallas kernels for 0% -> 0%
where the time goes in v1:
time: 365 us; the launch traced here: 364 us
  waiting for transfers between devices  194 us (53%)
  local copies, waits for them, and re-layouts  84.4 us (23%)
  matrix products  34.5 us (9%)
  blocking collectives  16.3 us (4%)
  between operations  13.9 us (4%)
  other arithmetic  11 us (3%)
  starting transfers between devices  9.13 us (3%)
    all_gather x1, waiting for transfers between devices, shards(): rows = lax.all_gather(got, GROUP, axis=1, tiled=True)  64.2 us
    reduce_scatter x1, waiting for transfers between devices, shards(): summed = lax.psum_scatter(terms, GROUP, scatter_dimension=0, tiled=True)  57 us
    slice x1, local copies, waits for them, and re-layouts, shards(): rows_s = rows[1].reshape(-1, model_width)  53.6 us
    all_gather x1, waiting for transfers between devices, shards(): plane = lax.all_gather(home, GROUP, axis=0, tiled=True)  43.9 us
    all_to_all x1, waiting for transfers between devices, shards(): lax.all_to_all(jnp.stack([stacked] * lax.axis_size('expert')), 'expert',...  29.1 us
    all_to_all x1, blocking collectives, shards(): lax.all_to_all(send, 'expert', split_axis=0, concat_axis=0, tiled=True)  16.3 us
    dot_general x3, matrix products, contract_rows(): lax.dot_general(left_side, right_side, (((0,), (0,)), ((), ())), preferre...  11.2 us
    another operation x1, local copies, waits for them, and re-layouts, shards(): rows_x = rows[0].reshape(-1, model_width)  10 us
  transfers between devices with their start and end apart: 4, of which 4 were waited for; matrix products, arithmetic and copies ran while one was open for 5% of the time, Pallas kernels for 0%

profile of v1, /device:TPU:1, one launch (start us, length us, event | category | flops | bytes accessed | tf_op | source)
XLA Modules:
  0.0 363.5 jit_solution(15917415698415318844)
XLA Ops:
  7.8 1.3 broadcast_select_fusion
  9.3 1.5 fusion.43
  11.9 1.9 stack.4
  13.8 9.0 %all-to-all-start = ((bf16[8,256,768]{2,1,0:T(8,128)(2,1)}), bf16[8,256,768]{2,1,0:T(8,128)(2,1)S(1)}, u32[]{:S(2)}, u32[]{:S(2)}) async-start(bf16[8,256,768]{2,1,0:T(8,128)(2,1)} %stack.4), calls=%async_computation | async-start | bytes 6291456 | tf_op jit(solution)/shard_map/all_to_all | solution.py:49
  22.8 43.9 %all-gather.3.cloned.1.call-done = bf16[512,4224]{1,0:T(8,128)(2,1)} async-done(((bf16[16,4224]{1,0:T(8,128)(2,1)}), bf16[512,4224]{1,0:T(8,128)(2,1)}) %all-gather.3.cloned.1.call-update) | async-done | bytes 4325392 | tf_op jit(solution)/shard_map/all_gather | solution.py:58
  68.0 29.1 %all-to-all-done = bf16[8,256,768]{2,1,0:T(8,128)(2,1)S(1)} async-done(((bf16[8,256,768]{2,1,0:T(8,128)(2,1)}), bf16[8,256,768]{2,1,0:T(8,128)(2,1)S(1)}, u32[]{:S(2)}, u32[]{:S(2)}) %all-to-all-start) | async-done | bytes 3145760 | tf_op jit(solution)/shard_map/all_to_all | solution.py:49
  97.0 2.5 fusion.16
  106.0 2.6 pad_maximum_fusion
  110.9 1.9 convolution_convert_fusion.4
  116.3 1.7 stack_reshape.6
  119.4 16.3 %all_to_all.10 = bf16[8,2,5,2048]{3,1,2,0:T(2,128)(2,1)} all-to-all(bf16[8,2,5,2048]{3,1,2,0:T(2,128)(2,1)S(1)} %copy.25), channel_id=1, replica_groups=mesh['dp'=8,'expert'=8,'tensor'=4] {'expert'}, dimensions={0} | all-to-all | bytes 655360 | tf_op jit(solution)/shard_map/all_to_all | solution.py:100
  135.8 57.0 %reduce-scatter.2.cloned.1.call-done = bf16[16,4096]{1,0:T(8,128)(2,1)} async-done(((bf16[512,4096]{1,0:T(8,128)(2,1)}), bf16[16,4096]{1,0:T(8,128)(2,1)}) %reduce-scatter.2.cloned.1.call-update) | async-done | bytes 131088 | tf_op jit(solution)/shard_map/reduce_scatter | solution.py:72
  192.8 1.5 slice.86
  194.3 1.5 multiply_convert_fusion.14
  195.8 64.2 %all-gather.5.cloned.1.call-done = bf16[2,256,5,2048]{3,0,2,1:T(2,128)(2,1)} async-done(((bf16[2,8,5,2048]{3,0,2,1:T(2,128)(2,1)}), bf16[2,256,5,2048]{3,0,2,1:T(2,128)(2,1)}) %all-gather.5.cloned.1.call-update) | async-done | bytes 10485776 | tf_op jit(solution)/shard_map/all_gather | solution.py:102
  260.0 53.6 %slice_reduce_fusion = (bf16[256,5,2048]{2,1,0:T(8,128)(2,1)}, bf16[256,5,2048]{2,1,0:T(8,128)(2,1)}) fusion(bf16[2,256,5,2048]{3,0,2,1:T(2,128)(2,1)} %all-gather.5.cloned.1.call-done), kind=kLoop, calls=%fused_computation | loop fusion | bytes 20971520 | tf_op jit(solution)/shard_map/slice | solution.py:104
  313.6 10.0 %reshape_squeeze.6 = bf16[1280,2048]{1,0:T(8,128)(2,1)} reshape(bf16[256,5,2048]{2,1,0:T(8,128)(2,1)} %get-tuple-element.18) | data formatting | bytes 10485760 | tf_op jit(solution)/shard_map/reshape;squeeze | solution.py:103
  323.7 5.2 %fusion.24 = f32[1280,256]{1,0:T(8,128)} fusion(bf16[1280,2048]{1,0:T(8,128)(2,1)} %reshape_squeeze.6, bf16[2048,768]{1,0:T(8,128)(2,1)S(1)} %bitcast.24), kind=kOutput, calls=%fused_computation.38 | convolution fusion | flops 1342177280 | bytes 7602176 | tf_op jit(solution)/shard_map/dot_general | solution.py:27
  328.9 2.6 fusion.21
  331.5 10.0 %reshape_squeeze.7 = bf16[1280,2048]{1,0:T(8,128)(2,1)} reshape(bf16[256,5,2048]{2,1,0:T(8,128)(2,1)} %get-tuple-element.17) | data formatting | bytes 10485760 | tf_op jit(solution)/shard_map/reshape;squeeze | solution.py:104
  341.5 4.2 %fusion.27 = f32[1280,256]{1,0:T(8,128)S(1)} fusion(bf16[1280,2048]{1,0:T(8,128)(2,1)} %reshape_squeeze.7, bf16[2048,768]{1,0:T(8,128)(2,1)S(1)} %bitcast.26), kind=kOutput, calls=%fused_computation.41 | convolution fusion | flops 1342177280 | bytes 7602176 | tf_op jit(solution)/shard_map/dot_general | solution.py:35
  345.8 5.4 %fusion.4 = bf16[1,2048,256]{2,1,0:T(8,128)(2,1)} fusion(bf16[1280,2048]{1,0:T(8,128)(2,1)} %reshape_squeeze.7, f32[1280,256]{1,0:T(8,128)S(1)} %copy-done.7, f32[1280,256]{1,0:T(8,128)S(1)} %copy-done.6), kind=kOutput, calls=%fused_computation.14 | convolution fusion | flops 1344667648 | bytes 8912896 | tf_op jit(solution)/shard_map/dot_general | solution.py:15
  351.2 2.9 fusion.3
  354.0 3.0 fusion.2
  (56 shorter events, 16.8 us)
Async XLA Ops:
  7.2 59.6 %all-gather.3.cloned.1.call-start = ((), (), s32[]{:S(2)}) async-start(), calls=%async_computation.3 | async-start | bytes 4460544 | tf_op jit(solution)/shard_map/all_gather | solution.py:58
  13.8 83.3 %all-to-all-start = ((bf16[8,256,768]{2,1,0:T(8,128)(2,1)}), bf16[8,256,768]{2,1,0:T(8,128)(2,1)S(1)}, u32[]{:S(2)}, u32[]{:S(2)}) async-start(bf16[8,256,768]{2,1,0:T(8,128)(2,1)} %stack.4), calls=%async_computation | async-start | bytes 6291456 | tf_op jit(solution)/shard_map/all_to_all | solution.py:49
  22.8 170.0 %reduce-scatter.2.cloned.1.call-start = ((), (), s32[]{:S(2)}) async-start(), calls=%async_computation.4 | async-start | bytes 4325376 | tf_op jit(solution)/shard_map/reduce_scatter | solution.py:72
  97.0 2.9 copy-start.4
  108.5 0.7 copy-start.5
  108.5 0.9 copy-start.3
  108.5 1.0 copy-start.1
  108.5 5.2 %copy-start.2 = (bf16[16,2048]{1,0:T(8,128)(2,1)S(1)}, bf16[16,2048]{1,0:T(8,128)(2,1)}, u32[]{:S(2)}) copy-start(bf16[16,2048]{1,0:T(8,128)(2,1)} %param.9) | copy-start | bytes 196612
  108.6 151.5 %all-gather.5.cloned.1.call-start = ((), (), s32[]{:S(2)}) async-start(), calls=%async_computation.5 | async-start | bytes 10813440 | tf_op jit(solution)/shard_map/all_gather | solution.py:102
  323.7 5.2 %copy-start = (bf16[1280,2048]{1,0:T(8,128)(2,1)S(1)}, bf16[1280,2048]{1,0:T(8,128)(2,1)}, u32[]{:S(2)}) copy-start(bf16[1280,2048]{1,0:T(8,128)(2,1)} %reshape_squeeze.6) | copy-start | bytes 15728644
  341.5 4.2 %copy-start.6 = (f32[1280,256]{1,0:T(8,128)S(1)}, f32[1280,256]{1,0:T(8,128)}, u32[]{:S(2)}) copy-start(f32[1280,256]{1,0:T(8,128)} %fusion.24) | copy-start | bytes 3932164
  341.5 4.2 %copy-start.7 = (f32[1280,256]{1,0:T(8,128)S(1)}, f32[1280,256]{1,0:T(8,128)}, u32[]{:S(2)}) copy-start(f32[1280,256]{1,0:T(8,128)} %fusion.21) | copy-start | bytes 3932164
  341.5 9.6 %slice-start = ((s8[5242880]{0:T(1024)(128)(4,1)}), s8[4194304]{0:T(1024)(128)(4,1)S(1)}, s32[]{:S(2)}) async-start(s8[5242880]{0:T(1024)(128)(4,1)} %bitcast.27), calls=%async_computation.6 | async-start | bytes 8388608
  345.8 5.4 %slice-start.1 = ((s8[5242880]{0:T(1024)(128)(4,1)}), s8[1048576]{0:T(1024)(128)(4,1)S(1)}, s32[]{:S(2)}) async-start(s8[5242880]{0:T(1024)(128)(4,1)} %bitcast.27), calls=%async_computation.7 | async-start | bytes 2097152
Sparse Core Ops, SparseCore 0:
  11.2 55.5 all-gather.2
  108.7 84.0 reduce-scatter.1
  195.7 64.3 all-gather.4
